TPU v7x, 128 devices: a whole 4x4x4 slice. The times are simulated.
128 devices in a mesh: req: 32 (over z, y, core), seq: 4 (over x).
Axes of the slice: x: 4, y: 4, z: 4, core: 2. Of those that a mesh axis runs over, the one named last changes fastest.
Arguments:
- hidden: bfloat16 [32, 4, 512, 2048], P('req', 'seq'), may hold values from -6 to 6
- w_in: bfloat16 [2048, 4384], P('req', 'seq'), may hold values from -0.125 to 0.125
- conv_weight: float32 [4, 2304], replicated, may hold values from -3 to 3
- conv_bias: float32 [2304], replicated, may hold values from -0.5 to 0.5
- dt_bias: float32 [32], replicated, may hold values from -5 to -2
- a_log: float32 [32], replicated, may hold values from -12 to 2
- d_skip: float32 [32], replicated, may hold values from 0.5 to 1.5
- norm_weight: float32 [2048], replicated, may hold values from 0.5 to 1.5
- lengths: int32 [32], replicated, may hold values from 4 to 512, as said below
- prompt_group: int32 [32], replicated, may hold values from 0 to 31, each once
Outputs:
- gated_out: bfloat16 [32, 4, 512, 2048], P('req', 'seq')
- final_states: float32 [32, 32, 64, 128], P(None, 'req', 'seq')
Inputs may be any that keep to these rules, and one draw needn't show every extreme that they name: Every prompt has 4 * lengths[p] tokens; some prompt has exactly 512 a device. Group prompt_group[p] holds prompt p; each group holds one prompt.
All inputs are finite; a program needn't handle non-finite values.
Results may differ from a plain program's by a relative error of at most 0.0059.
Values may be sent and summed in bfloat16 or wider, within the bound.
No kernel may reach another device: no remote copies, remote signals or barrier semaphores. Data moves between devices by JAX's collectives and lax.ppermute only.
A program may use at most 128 MiB of HBM per device.

v0:
```python
import jax
import jax.numpy as jnp
from jax import lax
from jax.sharding import PartitionSpec as P

BLOCK = 256


def shifted(block, axis, distance):
    devices = range(lax.axis_size(axis))
    route = [(i - distance, i) for i in devices if i - distance in devices]
    return lax.ppermute(block, axis, route)


def block_step(state, pieces):
    inputs_x, b_rows, c_rows, step_dt, log_decay = pieces
    length = inputs_x.shape[0]
    heads = step_dt.shape[1]
    hdim = inputs_x.shape[1] // heads
    running = jnp.cumsum(log_decay, axis=0)
    gram = jnp.einsum("tn,un->tu", c_rows, b_rows, preferred_element_type=jnp.float32)
    later = jnp.arange(length)[:, None] >= jnp.arange(length)[None, :]
    spread = running.T[:, :, None] - running.T[:, None, :]
    decay = jnp.where(later[None], jnp.exp(jnp.where(later[None], spread, 0.0)), 0.0)
    mixing = (gram[None] * decay * step_dt.T[:, None, :]).astype(jnp.bfloat16)
    heads_x = inputs_x.reshape(length, heads, hdim)
    inside = jnp.einsum("htu,uhp->thp", mixing, heads_x, preferred_element_type=jnp.float32)
    carried = jnp.exp(running)[:, :, None] * jnp.einsum(
        "tn,hpn->thp", c_rows.astype(jnp.float32), state, precision=lax.Precision.HIGHEST
    )
    final_log = running[-1]
    weighting = jnp.exp(final_log[None, :] - running) * step_dt
    weighted = (
        (heads_x.astype(jnp.float32) * weighting[:, :, None])
        .astype(jnp.bfloat16)
        .reshape(length, heads * hdim)
    )
    contrib = jnp.einsum("ud,un->dn", weighted, b_rows, preferred_element_type=jnp.float32).reshape(
        heads, hdim, -1
    )
    new_state = jnp.exp(final_log)[:, None, None] * state + contrib
    return (new_state, (inside + carried).reshape(length, heads * hdim))


def local(
    hidden, w_in, conv_weight, conv_bias, dt_bias, a_log, d_skip, norm_weight, lengths, prompt_group
):
    tok_rows = hidden[0, 0]
    slots = tok_rows.shape[0]
    inner = norm_weight.shape[0]
    heads = dt_bias.shape[0]
    hdim = inner // heads
    nstate = (conv_bias.shape[0] - inner) // 2
    convdim = conv_bias.shape[0]
    taps = conv_weight.shape[0]
    seq_count = lax.axis_size("seq")
    my_group = lax.axis_index("req")
    my_block = lax.axis_index("seq")
    qlen = jnp.sum(jnp.where(prompt_group == my_group, lengths, 0))
    filled = jnp.arange(slots, dtype=jnp.int32) < qlen
    wide_rows = lax.all_gather(w_in, "seq", axis=1, tiled=True)
    projected = jnp.dot(
        tok_rows,
        lax.all_gather(wide_rows, "req", axis=0, tiled=True),
        preferred_element_type=jnp.float32,
    ).astype(jnp.bfloat16)
    gate_z = projected[:, :inner]
    conv_in = projected[:, inner : inner + convdim]
    dt_raw = projected[:, inner + convdim :]
    edge_rows = lax.dynamic_slice_in_dim(conv_in, qlen - (taps - 1), taps - 1, 0)
    prev_edge = shifted(edge_rows, "seq", 1)
    extended = jnp.concatenate([prev_edge, conv_in], axis=0)
    accum = jnp.zeros((slots, convdim), jnp.float32) + conv_bias[None, :]
    for tap_index in range(taps):
        accum = accum + conv_weight[tap_index][None, :] * extended[
            tap_index : tap_index + slots
        ].astype(jnp.float32)
    conv_act = jax.nn.silu(accum).astype(jnp.bfloat16)
    inputs_x = conv_act[:, :inner]
    b_rows = conv_act[:, inner : inner + nstate]
    c_rows = conv_act[:, inner + nstate :]
    step_dt = jnp.where(
        filled[:, None], jax.nn.softplus(dt_raw.astype(jnp.float32) + dt_bias[None, :]), 0.0
    )
    log_decay = step_dt * (-jnp.exp(a_log))[None, :]
    through = jnp.cumsum(log_decay, axis=0)
    block_total = through[-1]
    block_rows = min(BLOCK, slots)
    count = slots // block_rows
    pieces = (
        inputs_x.reshape(count, block_rows, inner),
        b_rows.reshape(count, block_rows, nstate),
        c_rows.reshape(count, block_rows, nstate),
        step_dt.reshape(count, block_rows, heads),
        log_decay.reshape(count, block_rows, heads),
    )
    zero_state = jnp.zeros((heads, hdim, nstate), jnp.float32)
    local_end, outputs = lax.scan(block_step, zero_state, pieces)
    decays_all = lax.all_gather(block_total[None, :], "seq", axis=0, tiled=True)
    after_mine = jnp.sum(
        jnp.where(jnp.arange(seq_count)[:, None] > my_block, decays_all, 0.0), axis=0
    )
    entering = zero_state
    for turn in range(seq_count - 1):
        entering = shifted(jnp.exp(block_total)[:, None, None] * entering + local_end, "seq", 1)
    incoming = jnp.exp(through)[:, :, None] * jnp.einsum(
        "tn,hpn->thp", c_rows.astype(jnp.float32), entering, precision=lax.Precision.HIGHEST
    )
    heads_y = (
        outputs.reshape(slots, heads, hdim)
        + incoming
        + d_skip[None, :, None] * inputs_x.astype(jnp.float32).reshape(slots, heads, hdim)
    )
    gated = heads_y.reshape(slots, inner) * jax.nn.silu(gate_z.astype(jnp.float32))
    scale = lax.rsqrt(jnp.mean(gated * gated, axis=1, keepdims=True) + 1e-05)
    normed = jnp.where(filled[:, None], gated * scale * norm_weight[None, :], 0.0)
    gated_out = normed.astype(jnp.bfloat16).reshape(1, 1, slots, inner)
    decayed_end = jnp.exp(after_mine)[:, None, None] * local_end
    share = lax.psum_scatter(decayed_end, "seq", scatter_dimension=1, tiled=True)
    moved = lax.all_to_all(share[None], "req", split_axis=1, concat_axis=0, tiled=True)
    final_states = jnp.take(moved, prompt_group, axis=0)
    return (gated_out, final_states)


def solution(mesh):
    in_specs = (
        P("req", "seq", None, None),
        P("req", "seq"),
        P(),
        P(),
        P(),
        P(),
        P(),
        P(),
        P(),
        P(),
    )
    out_specs = (P("req", "seq", None, None), P(None, "req", "seq", None))
    return jax.shard_map(local, mesh=mesh, in_specs=in_specs, out_specs=out_specs, check_vma=False)
```

profile of v0, /device:TPU:7, one launch (start us, length us, event | category | flops | bytes accessed | tf_op | source)
XLA Modules:
  0.0 385.6 jit_solution(3540427270740208996)
XLA Ops:
  7.2 10.4 %all-gather = bf16[4,1096,64]{1,2,0:T(8,128)(2,1)S(1)} all-gather(bf16[1,1096,64]{1,2,0:T(8,128)(2,1)} %bitcast.173), channel_id=1, replica_groups=mesh['req'=32,'seq'=4] {'seq'}, dimensions={0}, use_global_device_ids=true | all-gather | bytes 701440 | tf_op jit(solution)/shard_map/all_gather | solution.py:61
  18.1 1.2 reshape.185
  19.4 1.3 compare_select_fusion.1
  22.7 1.0 slice_reduce_fusion.7
  23.7 0.7 exponential_negate_fusion
  24.4 77.4 %all-gather.4.cloned.1.call-done = bf16[2048,4384]{1,0:T(8,128)(2,1)} async-done(((bf16[64,4384]{1,0:T(8,128)(2,1)}), bf16[2048,4384]{1,0:T(8,128)(2,1)}) %all-gather.4.cloned.1.call-update) | async-done | bytes 17956880 | tf_op jit(solution)/shard_map/all_gather | solution.py:64
  101.8 15.3 %convolution_convert_fusion = bf16[512,4384]{0,1:T(8,128)(2,1)} fusion(bf16[2048,4384]{1,0:T(8,128)(2,1)} %all-gather.4.cloned.1.call-done, bf16[1,1,512,2048]{3,2,1,0:T(8,128)(2,1)S(1)} %copy-done), kind=kOutput, calls=%fused_computation.45 | convolution fusion | flops 9196158976 | bytes 24543232 | tf_op jit(solution)/shard_map/dot_general | solution.py:62
  117.1 1.8 slice.81
  119.0 1.4 copy-done.5
  120.9 1.5 collective-permute-start
  122.4 0.9 fusion.43
  123.3 1.2 reduce-window.16
  124.7 0.7 slice_reduce_fusion.3
  127.2 10.5 %multiply_convert_fusion.4 = bf16[512,2304]{0,1:T(8,128)(2,1)S(1)} fusion(bf16[512,2304]{0,1:T(8,128)(2,1)} %copy-done.5, bf16[3,2304]{0,1:T(8,128)(2,1)S(1)} %copy.57, f32[2304]{0:T(1024)S(1)} %get-tuple-element.118, f32[2304]{0:T(1024)S(1)} %get-tuple-element.119, f32[2304]{0:T(1024)S(1)} %get-tuple-element.117, f32[2304]{0:T(1024)S(1)} %get-tuple-element.116, ...), kind=kLoop, calls=%fused_computation.48 | loop fusion | flops 30670848 | bytes 4778496 | tf_op jit(solution)/shard_map/convert_element_type | solution.py:78
  137.8 0.9 fusion.44
  138.6 1.8 copy.104
  140.6 1.0 copy.71
  141.6 117.3 %while.13 = (s32[]{:T(128)}, f32[32,64,128]{2,1,0:T(8,128)S(1)}, f32[2,256,2048]{1,0,2:T(2,128)}, f32[2,256,32]{1,0,2:T(2,128)S(1)}, bf16[2,256,2048]{1,2,0:T(8,...) while((s32[]{:T(128)}, f32[32,64,128]{2,1,0:T(8,128)S(1)}, ...), condition=%wide.region_4.5_spmd.clone, body=%wide.region_1.4_spmd.clone.sunk | while | flops 1242128512 | bytes 25203156 | solution.py:98
  141.7 1.0 fusion.67
  142.7 0.9 constant_dynamic-slice_fusion.6
  144.8 1.5 fusion.66
  147.0 2.7 bitcast_add_fusion.2
  149.7 8.6 %copy.117 = f32[1,256,2048]{1,0,2:T(1,128)S(1)} copy(f32[1,256,2048]{1,2,0:T(8,128)S(1)} %bitcast.161) | data formatting | bytes 4194304 | tf_op jit(solution)/shard_map/while/body/jit(dynamic_update_index_in_dim)/dynamic_update_slice | solution.py:98
  158.3 42.0 %dynamic_update_slice.6 = f32[2,256,2048]{1,0,2:T(2,128)} dynamic-update-slice(f32[2,256,2048]{1,0,2:T(2,128)} %get-tuple-element.231, f32[1,256,2048]{1,0,2:T(1,128)S(1)} %copy.117, s32[]{:T(128)S(6)} %copy.122, s32[]{:T(128)} %constant.60.clone.1..sunk, s32[]{:T(128)} %constant.60.clone.1..sunk) | dynamic-update-slice | bytes 4194308 | tf_op jit(solution)/shard_map/while/body/jit(dynamic_update_index_in_dim)/dynamic_update_slice | solution.py:98
  200.3 1.0 fusion.67
  201.3 0.9 constant_dynamic-slice_fusion.6
  203.4 1.5 fusion.66
  205.7 2.7 bitcast_add_fusion.2
  208.4 8.6 %copy.117 = f32[1,256,2048]{1,0,2:T(1,128)S(1)} copy(f32[1,256,2048]{1,2,0:T(8,128)S(1)} %bitcast.161) | data formatting | bytes 4194304 | tf_op jit(solution)/shard_map/while/body/jit(dynamic_update_index_in_dim)/dynamic_update_slice | solution.py:98
  216.9 42.0 %dynamic_update_slice.6 = f32[2,256,2048]{1,0,2:T(2,128)} dynamic-update-slice(f32[2,256,2048]{1,0,2:T(2,128)} %get-tuple-element.231, f32[1,256,2048]{1,0,2:T(1,128)S(1)} %copy.117, s32[]{:T(128)S(6)} %copy.122, s32[]{:T(128)} %constant.60.clone.1..sunk, s32[]{:T(128)} %constant.60.clone.1..sunk) | dynamic-update-slice | bytes 4194308 | tf_op jit(solution)/shard_map/while/body/jit(dynamic_update_index_in_dim)/dynamic_update_slice | solution.py:98
  258.9 0.8 broadcast_add_fusion
  259.8 1.3 collective-permute-start.1
  261.1 27.8 %all-gather.1 = f32[4,1,32]{2,1,0:T(1,128)S(1)} all-gather(f32[1,1,32]{2,1,0:T(1,128)} %bitcast.175), channel_id=1, replica_groups=mesh['req'=32,'seq'=4] {'seq'}, dimensions={0}, use_global_device_ids=true | all-gather | bytes 640 | tf_op jit(solution)/shard_map/all_gather | solution.py:99
  289.0 1.2 broadcast_multiply_fusion
  290.2 1.3 collective-permute-start.2
  291.5 22.9 %collective-permute-done.2 = f32[32,64,128]{2,1,0:T(8,128)S(1)} collective-permute-done((f32[32,64,128]{2,1,0:T(8,128)S(1)}, f32[32,64,128]{2,1,0:T(8,128)S(1)}, u32[]{:S(2)}, u32[]{:S(2)}) %collective-permute-start.2) | collective-permute-done | bytes 1048608 | tf_op jit(solution)/shard_map/ppermute | solution.py:12
  314.4 1.2 multiply_add_fusion
  315.6 1.5 collective-permute-start.3
  317.3 6.4 %reshape.162 = f32[512,32,64]{0,2,1:T(8,128)} reshape(f32[2,256,2048]{1,0,2:T(2,128)} %get-tuple-element.45) | data formatting | bytes 8388608 | tf_op jit(solution)/shard_map/reshape | solution.py:110
  323.7 23.2 %collective-permute-done.3 = f32[32,64,128]{2,1,0:T(8,128)S(1)} collective-permute-done((f32[32,64,128]{2,1,0:T(8,128)}, f32[32,64,128]{2,1,0:T(8,128)S(1)}, u32[]{:S(2)}, u32[]{:S(2)}) %collective-permute-start.3) | collective-permute-done | bytes 1048608 | tf_op jit(solution)/shard_map/ppermute | solution.py:12
  347.0 2.7 fusion.37
  349.7 3.8 fusion.31
  353.5 1.9 copy-done.2
  355.4 3.0 multiply_reduce_fusion
  358.5 9.9 %all-to-all-start = ((f32[1,32,16,128]{3,2,0,1:T(8,128)}), f32[1,32,16,128]{3,2,0,1:T(8,128)S(1)}, u32[]{:S(2)}, u32[]{:S(2)}) async-start(f32[1,32,16,128]{3,2,0,1:T(8,128)} %bitcast.171), calls=%async_computation.1 | async-start | bytes 524288 | tf_op jit(solution)/shard_map/all_to_all | solution.py:120
  368.5 4.8 %fusion.34 = bf16[1,1,512,2048]{2,3,1,0:T(8,128)(2,1)} fusion(f32[2048]{0:T(1024)S(1)} %copy-done.12, f32[512]{0:T(512)S(1)} %add_rsqrt_fusion, pred[512]{0:T(512)(128)(4,1)S(1)} %iota_compare_fusion.1, bf16[512,4384]{0,1:T(8,128)(2,1)} %convolution_convert_fusion, f32[512,32,64]{0,2,1:T(8,128)} %copy-done.2), kind=kLoop, calls=%fused_computation.64 | loop fusion | flops 10485760 | bytes 8399360 | tf_op jit(solution)/shard_map/reshape | solution.py:117
  373.3 3.9 %copy.67 = bf16[1,1,512,2048]{3,2,1,0:T(8,128)(2,1)} copy(bf16[1,1,512,2048]{2,3,1,0:T(8,128)(2,1)} %fusion.34) | data formatting | bytes 4194304
  377.9 0.8 fusion.36
  (93 shorter events, 8.7 us)
Async XLA Ops:
  7.2 94.6 %copy-start = (bf16[1,1,512,2048]{3,2,1,0:T(8,128)(2,1)S(1)}, bf16[1,1,512,2048]{3,2,1,0:T(8,128)(2,1)}, u32[]{:S(2)}) copy-start(bf16[1,1,512,2048]{3,2,1,0:T(8,128)(2,1)} %param.12) | copy-start | bytes 6291460
  7.2 94.6 %all-gather.4.cloned.1.call-start = ((), (), s32[]{:S(2)}) async-start(), calls=%async_computation.2 | async-start | bytes 18923520 | tf_op jit(solution)/shard_map/all_gather | solution.py:64
  19.3 339.2 %reduce-scatter.2.cloned.1.call-start = ((), (), s32[]{:S(2)}) async-start(), calls=%async_computation.3 | async-start | bytes 1310720 | tf_op jit(solution)/shard_map/reduce_scatter | solution.py:119
  117.1 5.3 %copy-start.13 = (f32[32]{0:T(128)S(1)}, f32[32]{0:T(128)}, u32[]{:S(2)}) copy-start(f32[32]{0:T(128)} %param.16) | copy-start | bytes 388
  117.1 10.0 %copy-start.11 = (f32[2304]{0:T(1024)S(1)}, f32[2304]{0:T(1024)}, u32[]{:S(2)}) copy-start(f32[2304]{0:T(1024)} %param.15) | copy-start | bytes 27652
  119.0 1.4 copy-start.5
  120.9 5.9 %collective-permute-start = (bf16[3,2304]{1,0:T(4,128)(2,1)S(1)}, bf16[3,2304]{1,0:T(4,128)(2,1)S(1)}, u32[]{:S(2)}, u32[]{:S(2)}) collective-permute-start(bf16[3,2304]{1,0:T(4,128)(2,1)S(1)} %copy.56), channel_id=1, source_target_pairs={{0,1},{1,2},{2,3},{4,5},{5,6},{6,7},{8,9},{9,10},{10,11},{12,13},{... | collective-permute-start | bytes 41480 | tf_op jit(solution)/shard_map/ppermute | solution.py:12
  124.4 2.4 copy-start.7
  137.6 2.9 copy-start.6
  137.8 3.9 %copy-start.3 = (bf16[512,2048]{0,1:T(8,128)(2,1)}, bf16[512,2048]{0,1:T(8,128)(2,1)S(1)}, u32[]{:S(2)}) copy-start(bf16[512,2048]{0,1:T(8,128)(2,1)S(1)} %slice.86) | copy-start | bytes 6291460
  141.6 1.9 copy-start.9
  149.7 50.6 %copy-start.10 = (f32[2,256,32]{1,0,2:T(2,128)S(1)}, f32[2,256,32]{1,0,2:T(2,128)}, u32[]{:S(2)}) copy-start(f32[2,256,32]{1,0,2:T(2,128)} %copy-done.9) | copy-start | bytes 196612 | tf_op jit(solution)/shard_map/while
  200.3 1.9 copy-start.9
  208.4 50.6 %copy-start.10 = (f32[2,256,32]{1,0,2:T(2,128)S(1)}, f32[2,256,32]{1,0,2:T(2,128)}, u32[]{:S(2)}) copy-start(f32[2,256,32]{1,0,2:T(2,128)} %copy-done.9) | copy-start | bytes 196612 | tf_op jit(solution)/shard_map/while
  259.8 57.4 %copy-start.15 = (s32[32]{0:T(128)S(1)}, s32[32]{0:T(128)}, u32[]{:S(2)}) copy-start(s32[32]{0:T(128)} %param.21) | copy-start | bytes 388
  259.8 29.2 %collective-permute-start.1 = (f32[32,64,128]{2,1,0:T(8,128)S(1)}, f32[32,64,128]{2,1,0:T(8,128)S(1)}, u32[]{:S(2)}, u32[]{:S(2)}) collective-permute-start(f32[32,64,128]{2,1,0:T(8,128)S(1)} %broadcast_add_fusion), channel_id=1, source_target_pairs={{0,1},{1,2},{2,3},{4,5},{5,6},{6,7},{8,9},{9,10},{10,11},{12,13},{... | collective-permute-start | bytes 3145736 | tf_op jit(solution)/shard_map/ppermute | solution.py:12
  289.0 28.2 %copy-start.8 = (f32[32,4,128]{2,0,1:T(8,128)S(1)}, f32[32,4,128]{2,0,1:T(8,128)}, u32[]{:S(2)}) copy-start(f32[32,4,128]{2,0,1:T(8,128)} %copy-done.7) | copy-start | bytes 196612
  290.2 24.2 %collective-permute-start.2 = (f32[32,64,128]{2,1,0:T(8,128)S(1)}, f32[32,64,128]{2,1,0:T(8,128)S(1)}, u32[]{:S(2)}, u32[]{:S(2)}) collective-permute-start(f32[32,64,128]{2,1,0:T(8,128)S(1)} %get-tuple-element.150), channel_id=1, source_target_pairs={{0,1},{1,2},{2,3},{4,5},{5,6},{6,7},{8,9},{9,10},{10,11},{12,13},{... | collective-permute-start | bytes 3145736 | tf_op jit(solution)/shard_map/ppermute | solution.py:12
  315.6 31.3 %collective-permute-start.3 = (f32[32,64,128]{2,1,0:T(8,128)}, f32[32,64,128]{2,1,0:T(8,128)S(1)}, u32[]{:S(2)}, u32[]{:S(2)}) collective-permute-start(f32[32,64,128]{2,1,0:T(8,128)} %multiply_add_fusion), channel_id=1, source_target_pairs={{0,1},{1,2},{2,3},{4,5},{5,6},{6,7},{8,9},{9,10},{10,11},{12,13},{... | collective-permute-start | bytes 3145736 | tf_op jit(solution)/shard_map/ppermute | solution.py:12
  323.7 25.9 %copy-start.4 = (bf16[512,2048]{0,1:T(8,128)(2,1)S(1)}, bf16[512,2048]{0,1:T(8,128)(2,1)}, u32[]{:S(2)}) copy-start(bf16[512,2048]{0,1:T(8,128)(2,1)} %copy-done.3) | copy-start | bytes 6291460
  323.7 25.9 %copy-start.14 = (f32[32]{0:T(128)S(1)}, f32[32]{0:T(128)}, u32[]{:S(2)}) copy-start(f32[32]{0:T(128)} %param.18) | copy-start | bytes 388
  353.5 1.9 copy-start.2
  355.4 13.0 %copy-start.12 = (f32[2048]{0:T(1024)S(1)}, f32[2048]{0:T(1024)}, u32[]{:S(2)}) copy-start(f32[2048]{0:T(1024)} %param.19) | copy-start | bytes 24580
  358.5 18.8 %all-to-all-start = ((f32[1,32,16,128]{3,2,0,1:T(8,128)}), f32[1,32,16,128]{3,2,0,1:T(8,128)S(1)}, u32[]{:S(2)}, u32[]{:S(2)}) async-start(f32[1,32,16,128]{3,2,0,1:T(8,128)} %bitcast.171), calls=%async_computation.1 | async-start | bytes 524288 | tf_op jit(solution)/shard_map/all_to_all | solution.py:120
  368.5 10.3 %copy-start.1 = (bf16[1,1,512,2048]{3,2,1,0:T(8,128)(2,1)S(1)}, bf16[1,1,512,2048]{3,2,1,0:T(8,128)(2,1)}, u32[]{:S(2)}) copy-start(bf16[1,1,512,2048]{3,2,1,0:T(8,128)(2,1)} %param.12) | copy-start | bytes 6291460
Sparse Core Ops, SparseCore 0:
  19.4 82.3 all-gather.3
  317.3 31.4 reduce-scatter.1
where the time goes:
time: 392 us; the launch traced here: 386 us
  local copies, waits for them, and re-layouts  129 us (33%)
  waiting for transfers between devices  124 us (32%)
  blocking collectives  38.1 us (10%)
  other arithmetic  36.4 us (9%)
  matrix products  26.7 us (7%)
  between operations  15.7 us (4%)
  starting transfers between devices  15.5 us (4%)
    dynamic_update_slice x4, local copies, waits for them, and re-layouts, local(): local_end, outputs = lax.scan(block_step, zero_state, pieces)  101 us
    all_gather x1, waiting for transfers between devices, local(): lax.all_gather(wide_rows, 'req', axis=0, tiled=True)  77.4 us
    ppermute x4, waiting for transfers between devices, shifted(): return lax.ppermute(block, axis, route)  46.2 us
    all_gather x1, blocking collectives, local(): decays_all = lax.all_gather(block_total[None, :], 'seq', axis=0, tiled=True)  27.8 us
    dot_general x1, matrix products, local(): jnp.dot(tok_rows, lax.all_gather(wide_rows, 'req', axis=0, tiled=True), p...  15.3 us
    convert_element_type x1, other arithmetic, local(): conv_act = jax.nn.silu(accum).astype(jnp.bfloat16)  10.5 us
    all_gather x1, blocking collectives, local(): wide_rows = lax.all_gather(w_in, 'seq', axis=1, tiled=True)  10.4 us
    all_to_all x1, starting transfers between devices, local(): lax.all_to_all(share[None], 'req', split_axis=1, concat_axis=0, tiled=True)  9.92 us
  transfers between devices with their start and end apart: 7, of which 4 were waited for; matrix products, arithmetic and copies ran while one was open for 9% of the time, Pallas kernels for 0%

commit v1 on v0

--- a/solution.py
+++ b/solution.py
@@ -2,6 +2,7 @@
 import jax.numpy as jnp
 from jax import lax
 from jax.sharding import PartitionSpec as P
+from jax.lax import axis_index, ppermute, psum
 
 BLOCK = 256
 
@@ -58,7 +59,16 @@
     my_block = lax.axis_index("seq")
     qlen = jnp.sum(jnp.where(prompt_group == my_group, lengths, 0))
     filled = jnp.arange(slots, dtype=jnp.int32) < qlen
-    wide_rows = lax.all_gather(w_in, "seq", axis=1, tiled=True)
+    n_parts = psum(1, "seq")
+    q_next = [(hop_no - 1, hop_no) for hop_no in range(1, n_parts)] + [(n_parts - 1, 0)]
+    x_now = w_in
+    vals = [x_now]
+    for _ in tuple(range(n_parts - 1)):
+        x_now = ppermute(x_now, "seq", q_next)
+        vals += [x_now]
+    reached = jnp.concatenate([*reversed(vals)], 1)
+    back = axis_index("seq")
+    wide_rows = jnp.roll(reached, (back + 1) * x_now.shape[1], 1)
     projected = jnp.dot(
         tok_rows,
         lax.all_gather(wide_rows, "req", axis=0, tiled=True),

time: 392 us -> 397 us (1.013)
  waiting for transfers between devices: 124 us -> 135 us
  blocking collectives: 38.1 us -> 27.8 us
    all_gather x1 -> x0, blocking collectives: 10.4 us -> none  [local(): wide_rows = lax.all_gather(w_in, 'seq', axis=1, tiled=True)]
    ppermute x0 -> x3, waiting for transfers between devices: none -> 9.92 us  [local(): x_now = ppermute(x_now, 'seq', q_next)]
    unnamed x32 -> x33, local copies, waits for them, and re-layouts: 9.68 us -> 10.6 us
  transfers between devices with their start and end apart: 7 -> 10, of which waited for: 4 -> 7; matrix products, arithmetic and copies ran while one was open for 9% -> 8% of each run, Pallas kernels for 0% -> 0%
where the time goes in v1:
time: 397 us; the launch traced here: 390 us
  waiting for transfers between devices  135 us (34%)
  local copies, waits for them, and re-layouts  131 us (33%)
  other arithmetic  36.4 us (9%)
  blocking collectives  27.8 us (7%)
  matrix products  25.4 us (6%)
  starting transfers between devices  18.9 us (5%)
  between operations  15.7 us (4%)
    dynamic_update_slice x4, local copies, waits for them, and re-layouts, local(): local_end, outputs = lax.scan(block_step, zero_state, pieces)  101 us
    all_gather x1, waiting for transfers between devices, local(): lax.all_gather(wide_rows, 'req', axis=0, tiled=True)  78.2 us
    ppermute x4, waiting for transfers between devices, shifted(): return lax.ppermute(block, axis, route)  46.2 us
    all_gather x1, blocking collectives, local(): decays_all = lax.all_gather(block_total[None, :], 'seq', axis=0, tiled=True)  27.8 us
    dot_general x1, matrix products, local(): jnp.dot(tok_rows, lax.all_gather(wide_rows, 'req', axis=0, tiled=True), p...  14 us
    unnamed x33, local copies, waits for them, and re-layouts  10.6 us
    convert_element_type x1, other arithmetic, local(): conv_act = jax.nn.silu(accum).astype(jnp.bfloat16)  10.6 us
    ppermute x3, waiting for transfers between devices, local(): x_now = ppermute(x_now, 'seq', q_next)  9.92 us
  transfers between devices with their start and end apart: 10, of which 7 were waited for; matrix products, arithmetic and copies ran while one was open for 8% of the time, Pallas kernels for 0%

profile of v1, /device:TPU:7, one launch (start us, length us, event | category | flops | bytes accessed | tf_op | source)
XLA Modules:
  0.0 390.5 jit_solution(17807515857828950228)
XLA Ops:
  7.3 4.9 %collective-permute-done = bf16[64,1096]{1,0:T(8,128)(2,1)S(1)} collective-permute-done((bf16[64,1096]{1,0:T(8,128)(2,1)}, bf16[64,1096]{1,0:T(8,128)(2,1)S(1)}, u32[]{:S(2)}, u32[]{:S(2)}) %collective-permute-start) | collective-permute-done | bytes 140320 | tf_op jit(solution)/shard_map/ppermute | solution.py:67
  12.2 1.1 collective-permute-start.1
  13.3 2.9 collective-permute-done.1
  16.2 2.3 collective-permute-start.2
  18.5 2.1 collective-permute-done.2
  20.6 2.6 concatenate.9
  23.2 1.0 constant_dynamic-slice_fusion.4
  24.4 1.3 compare_select_fusion.1
  27.6 1.0 slice_reduce_fusion.7
  29.3 78.2 %all-gather.3.cloned.1.call-done = bf16[2048,4384]{1,0:T(8,128)(2,1)} async-done(((bf16[64,4384]{1,0:T(8,128)(2,1)}), bf16[2048,4384]{1,0:T(8,128)(2,1)}) %all-gather.3.cloned.1.call-update) | async-done | bytes 17956880 | tf_op jit(solution)/shard_map/all_gather | solution.py:74
  107.5 14.0 %fusion.27 = bf16[512,4384]{0,1:T(8,128)(2,1)S(1)} fusion(bf16[2048,4384]{1,0:T(8,128)(2,1)} %all-gather.3.cloned.1.call-done, bf16[1,1,512,2048]{3,2,1,0:T(8,128)(2,1)S(1)} %copy-done), kind=kOutput, calls=%fused_computation.46 | convolution fusion | flops 9196158976 | bytes 24543232 | tf_op jit(solution)/shard_map/dot_general | solution.py:72
  121.6 2.0 copy-done.7
  123.8 1.4 copy-done.5
  125.7 1.5 collective-permute-start.3
  128.1 1.2 reduce-window.16
  132.0 10.6 %multiply_convert_fusion.4 = bf16[512,2304]{0,1:T(8,128)(2,1)S(1)} fusion(bf16[512,2304]{0,1:T(8,128)(2,1)} %copy-done.5, bf16[3,2304]{0,1:T(8,128)(2,1)S(1)} %copy.54, f32[2304]{0:T(1024)S(1)} %get-tuple-element.118, f32[2304]{0:T(1024)S(1)} %get-tuple-element.119, f32[2304]{0:T(1024)S(1)} %get-tuple-element.117, f32[2304]{0:T(1024)S(1)} %get-tuple-element.116, ...), kind=kLoop, calls=%fused_computation.49 | loop fusion | flops 30670848 | bytes 4778496 | tf_op jit(solution)/shard_map/convert_element_type | solution.py:88
  142.7 0.9 fusion.45
  143.6 1.8 copy.101
  145.5 1.0 copy.68
  146.5 117.3 %while.13 = (s32[]{:T(128)}, f32[32,64,128]{2,1,0:T(8,128)S(1)}, f32[2,256,2048]{1,0,2:T(2,128)}, f32[2,256,32]{1,0,2:T(2,128)S(1)}, bf16[2,256,2048]{1,2,0:T(8,...) while((s32[]{:T(128)}, f32[32,64,128]{2,1,0:T(8,128)S(1)}, ...), condition=%wide.region_4.5_spmd.clone, body=%wide.region_1.4_spmd.clone.sunk | while | flops 1242128512 | bytes 25203156 | solution.py:108
  146.6 1.0 fusion.68
  147.6 0.9 constant_dynamic-slice_fusion.7
  149.7 1.5 fusion.67
  151.9 2.7 bitcast_add_fusion.2
  154.6 8.6 %copy.114 = f32[1,256,2048]{1,0,2:T(1,128)S(1)} copy(f32[1,256,2048]{1,2,0:T(8,128)S(1)} %bitcast.157) | data formatting | bytes 4194304 | tf_op jit(solution)/shard_map/while/body/jit(dynamic_update_index_in_dim)/dynamic_update_slice | solution.py:108
  163.2 42.0 %dynamic_update_slice.6 = f32[2,256,2048]{1,0,2:T(2,128)} dynamic-update-slice(f32[2,256,2048]{1,0,2:T(2,128)} %get-tuple-element.231, f32[1,256,2048]{1,0,2:T(1,128)S(1)} %copy.114, s32[]{:T(128)S(6)} %copy.119, s32[]{:T(128)} %constant.78.clone.1..sunk, s32[]{:T(128)} %constant.78.clone.1..sunk) | dynamic-update-slice | bytes 4194308 | tf_op jit(solution)/shard_map/while/body/jit(dynamic_update_index_in_dim)/dynamic_update_slice | solution.py:108
  205.2 1.0 fusion.68
  206.2 0.9 constant_dynamic-slice_fusion.7
  208.3 1.5 fusion.67
  210.6 2.7 bitcast_add_fusion.2
  213.3 8.6 %copy.114 = f32[1,256,2048]{1,0,2:T(1,128)S(1)} copy(f32[1,256,2048]{1,2,0:T(8,128)S(1)} %bitcast.157) | data formatting | bytes 4194304 | tf_op jit(solution)/shard_map/while/body/jit(dynamic_update_index_in_dim)/dynamic_update_slice | solution.py:108
  221.9 42.0 %dynamic_update_slice.6 = f32[2,256,2048]{1,0,2:T(2,128)} dynamic-update-slice(f32[2,256,2048]{1,0,2:T(2,128)} %get-tuple-element.231, f32[1,256,2048]{1,0,2:T(1,128)S(1)} %copy.114, s32[]{:T(128)S(6)} %copy.119, s32[]{:T(128)} %constant.78.clone.1..sunk, s32[]{:T(128)} %constant.78.clone.1..sunk) | dynamic-update-slice | bytes 4194308 | tf_op jit(solution)/shard_map/while/body/jit(dynamic_update_index_in_dim)/dynamic_update_slice | solution.py:108
  264.7 1.3 collective-permute-start.4
  266.0 27.8 %all-gather = f32[4,1,32]{2,1,0:T(1,128)S(1)} all-gather(f32[1,1,32]{2,1,0:T(1,128)} %bitcast.169), channel_id=1, replica_groups=mesh['req'=32,'seq'=4] {'seq'}, dimensions={0}, use_global_device_ids=true | all-gather | bytes 640 | tf_op jit(solution)/shard_map/all_gather | solution.py:109
  293.9 1.2 broadcast_multiply_fusion
  295.1 1.3 collective-permute-start.5
  296.4 22.9 %collective-permute-done.5 = f32[32,64,128]{2,1,0:T(8,128)S(1)} collective-permute-done((f32[32,64,128]{2,1,0:T(8,128)S(1)}, f32[32,64,128]{2,1,0:T(8,128)S(1)}, u32[]{:S(2)}, u32[]{:S(2)}) %collective-permute-start.5) | collective-permute-done | bytes 1048608 | tf_op jit(solution)/shard_map/ppermute | solution.py:13
  319.3 1.2 multiply_add_fusion
  320.5 1.5 collective-permute-start.6
  322.1 6.5 %reshape.162 = f32[512,32,64]{0,2,1:T(8,128)} reshape(f32[2,256,2048]{1,0,2:T(2,128)} %get-tuple-element.45) | data formatting | bytes 8388608 | tf_op jit(solution)/shard_map/reshape | solution.py:120
  328.6 23.2 %collective-permute-done.6 = f32[32,64,128]{2,1,0:T(8,128)S(1)} collective-permute-done((f32[32,64,128]{2,1,0:T(8,128)}, f32[32,64,128]{2,1,0:T(8,128)S(1)}, u32[]{:S(2)}, u32[]{:S(2)}) %collective-permute-start.6) | collective-permute-done | bytes 1048608 | tf_op jit(solution)/shard_map/ppermute | solution.py:13
  351.9 2.7 fusion.38
  354.6 3.8 fusion.32
  358.4 2.0 copy-done.2
  360.4 3.0 multiply_reduce_fusion
  363.5 9.9 %all-to-all-start = ((f32[1,32,16,128]{3,2,0,1:T(8,128)}), f32[1,32,16,128]{3,2,0,1:T(8,128)S(1)}, u32[]{:S(2)}, u32[]{:S(2)}) async-start(f32[1,32,16,128]{3,2,0,1:T(8,128)} %bitcast.166), calls=%async_computation.1 | async-start | bytes 524288 | tf_op jit(solution)/shard_map/all_to_all | solution.py:130
  373.4 4.8 %fusion.35 = bf16[1,1,512,2048]{2,3,1,0:T(8,128)(2,1)} fusion(f32[2048]{0:T(1024)S(1)} %copy-done.13, f32[512]{0:T(512)S(1)} %add_rsqrt_fusion, pred[512]{0:T(512)(128)(4,1)S(1)} %iota_compare_fusion.1, bf16[512,4384]{0,1:T(8,128)(2,1)} %copy-done.7, f32[512,32,64]{0,2,1:T(8,128)} %copy-done.2), kind=kLoop, calls=%fused_computation.65 | loop fusion | flops 10485760 | bytes 8399360 | tf_op jit(solution)/shard_map/reshape | solution.py:127
  378.1 3.9 %copy.64 = bf16[1,1,512,2048]{3,2,1,0:T(8,128)(2,1)} copy(bf16[1,1,512,2048]{2,3,1,0:T(8,128)(2,1)} %fusion.35) | data formatting | bytes 4194304
  (100 shorter events, 12.4 us)
Async XLA Ops:
  7.2 100.4 %copy-start = (bf16[1,1,512,2048]{3,2,1,0:T(8,128)(2,1)S(1)}, bf16[1,1,512,2048]{3,2,1,0:T(8,128)(2,1)}, u32[]{:S(2)}) copy-start(bf16[1,1,512,2048]{3,2,1,0:T(8,128)(2,1)} %param.12) | copy-start | bytes 6291460
  7.2 100.3 %all-gather.3.cloned.1.call-start = ((), (), s32[]{:S(2)}) async-start(), calls=%async_computation.2 | async-start | bytes 18923520 | tf_op jit(solution)/shard_map/all_gather | solution.py:74
  7.2 5.0 %collective-permute-start = (bf16[64,1096]{1,0:T(8,128)(2,1)}, bf16[64,1096]{1,0:T(8,128)(2,1)S(1)}, u32[]{:S(2)}, u32[]{:S(2)}) collective-permute-start(bf16[64,1096]{1,0:T(8,128)(2,1)} %param.13), channel_id=1, source_target_pairs={{0,1},{1,2},{2,3},{3,0},{4,5},{5,6},{6,7},{7,4},{8,9},{9,10},{10,1... | collective-permute-start | bytes 420872 | tf_op jit(solution)/shard_map/ppermute | solution.py:67
  12.2 4.0 %collective-permute-start.1 = (bf16[64,1096]{1,0:T(8,128)(2,1)S(1)}, bf16[64,1096]{1,0:T(8,128)(2,1)S(1)}, u32[]{:S(2)}, u32[]{:S(2)}) collective-permute-start(bf16[64,1096]{1,0:T(8,128)(2,1)S(1)} %collective-permute-done), channel_id=1, source_target_pairs={{0,1},{1,2},{2,3},{3,0},{4,5},{5,6},{6,7},{7,4},{8,9},{9,10},{10,1... | collective-permute-start | bytes 420872 | tf_op jit(solution)/shard_map/ppermute | solution.py:67
  16.2 4.4 %collective-permute-start.2 = (bf16[64,1096]{1,0:T(8,128)(2,1)S(1)}, bf16[64,1096]{1,0:T(8,128)(2,1)}, u32[]{:S(2)}, u32[]{:S(2)}) collective-permute-start(bf16[64,1096]{1,0:T(8,128)(2,1)S(1)} %collective-permute-done.1), channel_id=1, source_target_pairs={{0,1},{1,2},{2,3},{3,0},{4,5},{5,6},{6,7},{7,4},{8,9},{9,10},{10,1... | collective-permute-start | bytes 420872 | tf_op jit(solution)/shard_map/ppermute | solution.py:67
  24.3 339.2 %reduce-scatter.2.cloned.1.call-start = ((), (), s32[]{:S(2)}) async-start(), calls=%async_computation.3 | async-start | bytes 1310720 | tf_op jit(solution)/shard_map/reduce_scatter | solution.py:129
  121.5 2.1 copy-start.7
  123.6 3.6 copy-start.14
  123.6 8.4 %copy-start.12 = (f32[2304]{0:T(1024)S(1)}, f32[2304]{0:T(1024)}, u32[]{:S(2)}) copy-start(f32[2304]{0:T(1024)} %param.15) | copy-start | bytes 27652
  123.8 1.5 copy-start.5
  125.7 5.9 %collective-permute-start.3 = (bf16[3,2304]{1,0:T(4,128)(2,1)S(1)}, bf16[3,2304]{1,0:T(4,128)(2,1)S(1)}, u32[]{:S(2)}, u32[]{:S(2)}) collective-permute-start(bf16[3,2304]{1,0:T(4,128)(2,1)S(1)} %copy.53), channel_id=1, source_target_pairs={{0,1},{1,2},{2,3},{4,5},{5,6},{6,7},{8,9},{9,10},{10,11},{12,13},{... | collective-permute-start | bytes 41480 | tf_op jit(solution)/shard_map/ppermute | solution.py:13
  129.3 2.3 copy-start.8
  142.5 2.9 copy-start.6
  142.7 3.9 copy-start.3
  146.6 1.9 copy-start.10
  154.6 50.6 %copy-start.11 = (f32[2,256,32]{1,0,2:T(2,128)S(1)}, f32[2,256,32]{1,0,2:T(2,128)}, u32[]{:S(2)}) copy-start(f32[2,256,32]{1,0,2:T(2,128)} %copy-done.10) | copy-start | bytes 196612 | tf_op jit(solution)/shard_map/while
  205.2 1.9 copy-start.10
  213.3 50.6 %copy-start.11 = (f32[2,256,32]{1,0,2:T(2,128)S(1)}, f32[2,256,32]{1,0,2:T(2,128)}, u32[]{:S(2)}) copy-start(f32[2,256,32]{1,0,2:T(2,128)} %copy-done.10) | copy-start | bytes 196612 | tf_op jit(solution)/shard_map/while
  264.7 57.3 %copy-start.16 = (s32[32]{0:T(128)S(1)}, s32[32]{0:T(128)}, u32[]{:S(2)}) copy-start(s32[32]{0:T(128)} %param.21) | copy-start | bytes 388
  264.7 29.2 %collective-permute-start.4 = (f32[32,64,128]{2,1,0:T(8,128)S(1)}, f32[32,64,128]{2,1,0:T(8,128)S(1)}, u32[]{:S(2)}, u32[]{:S(2)}) collective-permute-start(f32[32,64,128]{2,1,0:T(8,128)S(1)} %broadcast_add_fusion), channel_id=1, source_target_pairs={{0,1},{1,2},{2,3},{4,5},{5,6},{6,7},{8,9},{9,10},{10,11},{12,13},{... | collective-permute-start | bytes 3145736 | tf_op jit(solution)/shard_map/ppermute | solution.py:13
  293.9 28.2 %copy-start.9 = (f32[32,4,128]{2,0,1:T(8,128)S(1)}, f32[32,4,128]{2,0,1:T(8,128)}, u32[]{:S(2)}) copy-start(f32[32,4,128]{2,0,1:T(8,128)} %copy-done.8) | copy-start | bytes 196612
  295.1 24.2 %collective-permute-start.5 = (f32[32,64,128]{2,1,0:T(8,128)S(1)}, f32[32,64,128]{2,1,0:T(8,128)S(1)}, u32[]{:S(2)}, u32[]{:S(2)}) collective-permute-start(f32[32,64,128]{2,1,0:T(8,128)S(1)} %get-tuple-element.150), channel_id=1, source_target_pairs={{0,1},{1,2},{2,3},{4,5},{5,6},{6,7},{8,9},{9,10},{10,11},{12,13},{... | collective-permute-start | bytes 3145736 | tf_op jit(solution)/shard_map/ppermute | solution.py:13
  320.5 31.4 %collective-permute-start.6 = (f32[32,64,128]{2,1,0:T(8,128)}, f32[32,64,128]{2,1,0:T(8,128)S(1)}, u32[]{:S(2)}, u32[]{:S(2)}) collective-permute-start(f32[32,64,128]{2,1,0:T(8,128)} %multiply_add_fusion), channel_id=1, source_target_pairs={{0,1},{1,2},{2,3},{4,5},{5,6},{6,7},{8,9},{9,10},{10,11},{12,13},{... | collective-permute-start | bytes 3145736 | tf_op jit(solution)/shard_map/ppermute | solution.py:13
  328.6 25.9 %copy-start.4 = (bf16[512,2048]{0,1:T(8,128)(2,1)S(1)}, bf16[512,2048]{0,1:T(8,128)(2,1)}, u32[]{:S(2)}) copy-start(bf16[512,2048]{0,1:T(8,128)(2,1)} %copy-done.3) | copy-start | bytes 6291460
  328.6 25.9 %copy-start.15 = (f32[32]{0:T(128)S(1)}, f32[32]{0:T(128)}, u32[]{:S(2)}) copy-start(f32[32]{0:T(128)} %param.18) | copy-start | bytes 388
  358.4 2.0 copy-start.2
  360.4 12.9 %copy-start.13 = (f32[2048]{0:T(1024)S(1)}, f32[2048]{0:T(1024)}, u32[]{:S(2)}) copy-start(f32[2048]{0:T(1024)} %param.19) | copy-start | bytes 24580
  363.5 18.8 %all-to-all-start = ((f32[1,32,16,128]{3,2,0,1:T(8,128)}), f32[1,32,16,128]{3,2,0,1:T(8,128)S(1)}, u32[]{:S(2)}, u32[]{:S(2)}) async-start(f32[1,32,16,128]{3,2,0,1:T(8,128)} %bitcast.166), calls=%async_computation.1 | async-start | bytes 524288 | tf_op jit(solution)/shard_map/all_to_all | solution.py:130
  373.3 10.3 %copy-start.1 = (bf16[1,1,512,2048]{3,2,1,0:T(8,128)(2,1)S(1)}, bf16[1,1,512,2048]{3,2,1,0:T(8,128)(2,1)}, u32[]{:S(2)}) copy-start(bf16[1,1,512,2048]{3,2,1,0:T(8,128)(2,1)} %param.12) | copy-start | bytes 6291460
Sparse Core Ops, SparseCore 0:
  24.4 83.0 all-gather.2
  322.2 31.4 reduce-scatter.1
